TPU v7x, 256 devices: a whole 4x4x8 slice. The times are simulated.
256 devices in a mesh: seq: 32 (over z, y_lo, core), mp: 8 (over y_hi, x).
Axes of the slice: x: 4, y: 4 (y_hi: 2, y_lo: 2; y = y_hi * 2 + y_lo), z: 8, core: 2. Of those that a mesh axis runs over, the one named last changes fastest.
Arguments:
- tokens: bfloat16 [12288, 3072], P('seq', 'mp'), may hold values from -6 to 6
- w_qkv: bfloat16 [3072, 3, 3072], P(None, None, 'mp'), may hold values from -1 to 1
- q_gain: float32 [128], replicated, may hold values from 0 to 5
- k_gain: float32 [128], replicated, may hold values from 0 to 5
- w_out: bfloat16 [3072, 3072], P('mp'), may hold values from -0.15625 to 0.15625
- neighbours: int32 [32, 6], replicated, may hold values from 0 to 31, as said below
- counts: int32 [32], replicated, may hold values from 1 to 6
Outputs:
- mixed: bfloat16 [12288, 3072], P('seq', 'mp')
Inputs may be any that keep to these rules, and one draw needn't show every extreme that they name: `neighbours`: each row lists distinct tiles, each within 4 tiles of the row's own tile counted cyclically modulo 32.
All inputs are finite; a program needn't handle non-finite values.
Results may differ from a plain program's by a relative error of at most 0.014.
Values may be sent and summed in bfloat16 or wider, within the bound.
No kernel may reach another device: no remote copies, remote signals or barrier semaphores. Data moves between devices by JAX's collectives and lax.ppermute only.
A program may use at most 128 MiB of HBM per device.

v0:
```python
import jax
import jax.numpy as jnp
from jax import lax
from jax.sharding import PartitionSpec as P

HD = 128
TILE = 384
REACH = 4
NB = 6


def passed_along(value, axis, steps):
    count = lax.axis_size(axis)
    pairs = [(source, (source + steps) % count) for source in range(count)]
    return lax.ppermute(value, axis, pairs)


def head_norm(projected, gain_vec):
    per_head = projected.reshape(projected.shape[0], -1, HD)
    factor = lax.rsqrt(jnp.mean(per_head * per_head, axis=-1, keepdims=True) + 1e-06)
    return (per_head * factor * gain_vec).astype(jnp.bfloat16)


def on_device(tokens, w_qkv, q_gain, k_gain, w_out, neighbours, counts):
    tok_rows = tokens.shape[0]
    columns = w_qkv.shape[2]
    heads_here = columns // HD
    tiles_here = tok_rows // TILE
    total_tiles = neighbours.shape[0]
    span_here = (REACH + tiles_here - 1) // tiles_here
    flat_w = w_qkv.reshape(w_qkv.shape[0], 3 * columns)
    projected = jnp.dot(
        lax.all_gather(tokens, "mp", axis=1, tiled=True), flat_w, preferred_element_type=jnp.float32
    )
    queries = head_norm(projected[:, :columns], q_gain)
    key_part = head_norm(projected[:, columns : 2 * columns], k_gain).reshape(tok_rows, columns)
    value_part = projected[:, 2 * columns :].astype(jnp.bfloat16)
    paired = jnp.stack([key_part, value_part])
    blocks = []
    for offset in range(-span_here, span_here + 1):
        if offset == 0:
            blocks.append(paired)
        else:
            blocks.append(passed_along(paired, "seq", -offset))
    window = jnp.concatenate(blocks, axis=1)
    window_tiles = (2 * span_here + 1) * tiles_here
    position = lax.axis_index("seq")
    first_tile = position * tiles_here - span_here * tiles_here
    listed = lax.dynamic_slice_in_dim(neighbours, position * tiles_here, tiles_here, 0)
    used_counts = lax.dynamic_slice_in_dim(counts, position * tiles_here, tiles_here, 0)
    relative = jnp.mod(listed - first_tile, total_tiles)
    slot_used = jnp.arange(NB, dtype=jnp.int32)[None, :] < used_counts[:, None]
    query_blocks = queries.reshape(tiles_here, TILE, heads_here, HD)
    factor = HD ** (-0.5)
    hits = (
        relative[:, :, None] == jnp.arange(window_tiles, dtype=jnp.int32)[None, None, :]
    ) & slot_used[:, :, None]
    tile_mask = jnp.any(hits, axis=1)
    key_mask = jnp.repeat(tile_mask, TILE, axis=1)
    near_keys = window[0].reshape(window_tiles * TILE, heads_here, HD)
    near_values = window[1].reshape(window_tiles * TILE, heads_here, HD)
    scores = (
        jnp.einsum("tqhd,khd->thqk", query_blocks, near_keys, preferred_element_type=jnp.float32)
        * factor
    )
    scores = jnp.where(key_mask[:, None, None, :], scores, -jnp.inf)
    highest = jnp.max(scores, axis=-1, keepdims=True)
    expo = jnp.exp(scores - highest)
    probs = (expo / jnp.sum(expo, axis=-1, keepdims=True)).astype(jnp.bfloat16)
    attended = jnp.einsum("thqk,khd->tqhd", probs, near_values, preferred_element_type=jnp.float32)
    attended = attended.astype(jnp.bfloat16).reshape(tok_rows, columns)
    mixed_t = lax.psum_scatter(
        lax.dot_general(
            w_out, attended, (((0,), (1,)), ((), ())), preferred_element_type=jnp.float32
        ).astype(jnp.bfloat16),
        "mp",
        scatter_dimension=0,
        tiled=True,
    ).astype(jnp.float32)
    return mixed_t.T.astype(jnp.bfloat16)


def solution(mesh):
    return jax.shard_map(
        on_device,
        mesh=mesh,
        in_specs=(P("seq", "mp"), P(None, None, "mp"), P(), P(), P("mp", None), P(), P()),
        out_specs=P("seq", "mp"),
        check_vma=False,
    )
```

profile of v0, /device:TPU:2, one launch (start us, length us, event | category | flops | bytes accessed | tf_op | source)
XLA Modules:
  0.0 287.8 jit_solution(6885400218139403413)
XLA Ops:
  6.5 0.0 copy-start
  6.5 0.0 all-gather.2.cloned.1.call-start
  6.5 0.7 all-gather.2.cloned.1.call-update
  7.3 0.0 copy-start.5
  7.3 0.0 reduce-scatter.4.cloned.1.call-start
  7.3 10.3 %copy.31 = bf16[3072,3,384]{0,2,1:T(8,128)(2,1)} copy(bf16[3072,3,384]{2,0,1:T(8,128)(2,1)} %param.8) | data formatting | bytes 14155776 | tf_op args[1]
  17.6 0.0 copy-done.5
  17.6 59.3 %all-gather.2.cloned.1.call-done = bf16[384,3072]{1,0:T(8,128)(2,1)} async-done(((bf16[384,384]{1,0:T(8,128)(2,1)}), bf16[384,3072]{1,0:T(8,128)(2,1)}) %all-gather.2.cloned.1.call-update) | async-done | bytes 2359312 | tf_op jit(solution)/shard_map/all_gather | solution.py:33
  76.9 7.0 %fusion.21 = f32[384,1152]{1,0:T(8,128)S(1)} fusion(bf16[384,3072]{1,0:T(8,128)(2,1)} %all-gather.2.cloned.1.call-done, bf16[3072,1152]{0,1:T(8,128)(2,1)} %bitcast.63), kind=kOutput, calls=%fused_computation.47 | convolution fusion | flops 2717908992 | bytes 11206656 | tf_op jit(solution)/shard_map/dot_general | solution.py:32
  83.9 0.0 copy-start.2
  83.9 0.0 copy-start.6
  83.9 0.0 copy-start.4
  84.0 1.2 copy-done.2
  85.1 0.9 slice_multiply_fusion
  86.0 1.3 copy.32
  87.4 1.1 copy.33
  88.5 2.3 fusion.20
  90.9 0.9 pad_maximum_fusion
  91.7 1.6 collective-permute-start
  93.3 0.0 copy-done.6
  93.3 0.6 dynamic_slice.7
  93.9 0.0 copy-done.4
  93.9 0.2 fusion.14
  94.1 0.7 iota_compare_fusion.1
  94.7 0.1 collective-permute-start.1
  94.8 0.1 fusion.16
  94.9 0.1 broadcast_in_dim.12
  95.0 1.8 collective-permute-start.7
  96.9 1.3 collective-permute-start.3
  98.2 0.6 collective-permute-start.2
  98.7 1.3 copy.36
  100.0 0.1 multiply_reduce_fusion
  100.1 9.4 %collective-permute-done = bf16[2,384,384]{2,1,0:T(8,128)(2,1)} collective-permute-done((bf16[2,384,384]{2,1,0:T(8,128)(2,1)}, bf16[2,384,384]{2,1,0:T(8,128)(2,1)}, u32[]{:S(2)}, u32[]{:S(2)}) %collective-permute-start) | collective-permute-done | bytes 589856 | tf_op jit(solution)/shard_map/ppermute | solution.py:15
  109.5 0.0 collective-permute-start.4
  109.6 1.1 constant_dynamic-update-slice_fusion.8
  110.7 3.0 %collective-permute-done.1 = bf16[2,384,384]{2,1,0:T(8,128)(2,1)} collective-permute-done((bf16[2,384,384]{2,1,0:T(8,128)(2,1)}, bf16[2,384,384]{2,1,0:T(8,128)(2,1)}, u32[]{:S(2)}, u32[]{:S(2)}) %collective-permute-start.1) | collective-permute-done | bytes 589856 | tf_op jit(solution)/shard_map/ppermute | solution.py:15
  113.7 8.1 %collective-permute-start.5 = (bf16[2,384,384]{2,1,0:T(8,128)(2,1)}, bf16[2,384,384]{2,1,0:T(8,128)(2,1)S(1)}, u32[]{:S(2)}, u32[]{:S(2)}) collective-permute-start(bf16[2,384,384]{2,1,0:T(8,128)(2,1)} %pad_maximum_fusion), channel_id=1, source_target_pairs={{0,240},{8,248},{16,0},{24,8},{32,16},{40,24},{48,32},{56,40},{64,... | collective-permute-start | bytes 1769480 | tf_op jit(solution)/shard_map/ppermute | solution.py:15
  121.8 1.2 constant_dynamic-update-slice_fusion.7
  123.0 14.8 %collective-permute-done.2 = bf16[2,384,384]{2,1,0:T(8,128)(2,1)} collective-permute-done((bf16[2,384,384]{2,1,0:T(8,128)(2,1)}, bf16[2,384,384]{2,1,0:T(8,128)(2,1)}, u32[]{:S(2)}, u32[]{:S(2)}) %collective-permute-start.2) | collective-permute-done | bytes 589856 | tf_op jit(solution)/shard_map/ppermute | solution.py:15
  137.8 4.2 %collective-permute-start.6 = (bf16[2,384,384]{2,1,0:T(8,128)(2,1)}, bf16[2,384,384]{2,1,0:T(8,128)(2,1)S(1)}, u32[]{:S(2)}, u32[]{:S(2)}) collective-permute-start(bf16[2,384,384]{2,1,0:T(8,128)(2,1)} %pad_maximum_fusion), channel_id=1, source_target_pairs={{0,232},{8,240},{16,248},{24,0},{32,8},{40,16},{48,24},{56,32},{64... | collective-permute-start | bytes 1769480 | tf_op jit(solution)/shard_map/ppermute | solution.py:15
  141.9 1.2 constant_dynamic-update-slice_fusion.6
  143.1 0.0 collective-permute-done.3
  143.1 1.2 constant_dynamic-update-slice_fusion.5
  144.3 0.1 constant_dynamic-update-slice_fusion.4
  144.4 0.0 collective-permute-done.4
  144.4 0.1 constant_dynamic-update-slice_fusion.3
  144.5 13.7 %collective-permute-done.5 = bf16[2,384,384]{2,1,0:T(8,128)(2,1)S(1)} collective-permute-done((bf16[2,384,384]{2,1,0:T(8,128)(2,1)}, bf16[2,384,384]{2,1,0:T(8,128)(2,1)S(1)}, u32[]{:S(2)}, u32[]{:S(2)}) %collective-permute-start.5) | collective-permute-done | bytes 589856 | tf_op jit(solution)/shard_map/ppermute | solution.py:15
  158.3 0.1 constant_dynamic-update-slice_fusion.2
  158.4 2.9 %collective-permute-done.6 = bf16[2,384,384]{2,1,0:T(8,128)(2,1)S(1)} collective-permute-done((bf16[2,384,384]{2,1,0:T(8,128)(2,1)}, bf16[2,384,384]{2,1,0:T(8,128)(2,1)S(1)}, u32[]{:S(2)}, u32[]{:S(2)}) %collective-permute-start.6) | collective-permute-done | bytes 589856 | tf_op jit(solution)/shard_map/ppermute | solution.py:15
  161.2 0.1 constant_dynamic-update-slice_fusion.1
  161.3 0.0 collective-permute-done.7
  161.4 1.2 constant_dynamic-update-slice_fusion
  162.5 2.9 fusion.19
  165.4 4.5 %copy.35 = bf16[1,3456,384]{1,2,0:T(8,128)(2,1)} copy(bf16[1,3456,384]{2,1,0:T(8,128)(2,1)} %get-tuple-element.5) | data formatting | bytes 5308416 | tf_op jit(solution)/shard_map/slice | solution.py:60
  169.9 4.5 %copy.34 = bf16[1,3456,384]{1,2,0:T(8,128)(2,1)} copy(bf16[1,3456,384]{2,1,0:T(8,128)(2,1)} %get-tuple-element.6) | data formatting | bytes 5308416 | tf_op jit(solution)/shard_map/slice | solution.py:61
  174.5 5.7 %bitcast_reduce_fusion = (f32[3,384]{1,0:T(4,128)S(1)}, f32[3,3456,384]{2,1,0:T(8,128)S(1)}) fusion(pred[3456]{0:T(1024)(128)(4,1)S(1)} %broadcast_in_dim.13, bf16[3456,3,128]{0,2,1:T(8,128)(2,1)} %bitcast.62, f32[384,3,128]{0,2,1:T(8,128)S(1)} %bitcast.65, f32[128]{0:T(128)S(1)} %copy-done.3, f32[384,3]{0,1:T(4,128)S(1)} %add_rsqrt_fusion), kind=kOutput, calls=%fused_computation.1 | convolution fusion | flops 1031601024 | bytes 19182464 | tf_op jit(solution)/shard_map/tqhd,khd->thqk/dot_general | solution.py:63
  180.2 4.3 %fusion.1 = f32[3,384]{1,0:T(4,128)S(1)} fusion(f32[3,3456,384]{2,1,0:T(8,128)S(1)} %get-tuple-element.10, f32[3,384]{1,0:T(4,128)S(1)} %get-tuple-element.9, pred[3456]{0:T(1024)(128)(4,1)S(1)} %broadcast_in_dim.13), kind=kLoop, calls=%fused_computation.5 | loop fusion | flops 15924096 | bytes 15937920 | tf_op jit(solution)/shard_map/reduce_sum | solution.py:69
  184.5 4.7 %fusion.5 = bf16[3,128,384]{2,1,0:T(8,128)(2,1)S(1)} fusion(bf16[3456,3,128]{0,2,1:T(8,128)(2,1)S(1)} %bitcast.66, f32[3,384]{1,0:T(4,128)S(1)} %fusion.1, f32[3,384]{1,0:T(4,128)S(1)} %get-tuple-element.9, f32[3,3456,384]{2,1,0:T(8,128)S(1)} %get-tuple-element.10, pred[3456]{0:T(1024)(128)(4,1)S(1)} %broadcast_in_dim.13), kind=kOutput, calls=%fused_computation.10 | convolution fusion | flops 1039269888 | bytes 18887040 | tf_op jit(solution)/shard_map/thqk,khd->tqhd/dot_general | solution.py:70
  189.2 0.0 copy-done
  189.2 2.8 fusion.4
  192.1 4.3 %copy.43 = bf16[3072,384]{1,0:T(8,128)(2,1)} copy(bf16[3072,384]{0,1:T(8,128)(2,1)} %fusion.4) | data formatting | bytes 4718592
  196.3 0.0 reduce-scatter.4.cloned.1.call-update
  196.4 82.7 %reduce-scatter.4.cloned.1.call-done = bf16[384,384]{1,0:T(8,128)(2,1)} async-done(((bf16[3072,384]{1,0:T(8,128)(2,1)}), bf16[384,384]{1,0:T(8,128)(2,1)}) %reduce-scatter.4.cloned.1.call-update) | async-done | bytes 294928
  279.1 1.8 copy.44
  (11 shorter events, 0.2 us)
Async XLA Ops:
  6.5 182.7 %copy-start = (bf16[384,3072]{1,0:T(8,128)(2,1)S(1)}, bf16[384,3072]{1,0:T(8,128)(2,1)}, u32[]{:S(2)}) copy-start(bf16[384,3072]{1,0:T(8,128)(2,1)} %param.11) | copy-start | bytes 7077892
  6.5 70.4 %all-gather.2.cloned.1.call-start = ((), (), s32[]{:S(2)}) async-start(), calls=%async_computation.1 | async-start | bytes 2654208 | tf_op jit(solution)/shard_map/all_gather | solution.py:33
  7.3 10.3 %copy-start.5 = (f32[128]{0:T(128)S(1)}, f32[128]{0:T(128)}, u32[]{:S(2)}) copy-start(f32[128]{0:T(128)} %param.10) | copy-start | bytes 1540
  7.3 271.8 %reduce-scatter.4.cloned.1.call-start = ((), (), s32[]{:S(2)}) async-start(), calls=%async_computation.2 | async-start | bytes 2654208
  83.9 1.2 copy-start.2
  83.9 9.4 %copy-start.6 = (s32[32]{0:T(128)S(1)}, s32[32]{0:T(128)}, u32[]{:S(2)}) copy-start(s32[32]{0:T(128)} %param.13) | copy-start | bytes 388
  83.9 10.0 %copy-start.4 = (s32[32,6]{0,1:T(8,128)S(1)}, s32[32,6]{0,1:T(8,128)}, u32[]{:S(2)}) copy-start(s32[32,6]{0,1:T(8,128)} %param.12) | copy-start | bytes 2308
  91.7 17.8 %collective-permute-start = (bf16[2,384,384]{2,1,0:T(8,128)(2,1)}, bf16[2,384,384]{2,1,0:T(8,128)(2,1)}, u32[]{:S(2)}, u32[]{:S(2)}) collective-permute-start(bf16[2,384,384]{2,1,0:T(8,128)(2,1)} %pad_maximum_fusion), channel_id=1, source_target_pairs={{0,32},{8,40},{16,48},{24,56},{32,64},{40,72},{48,80},{56,88},{64,... | collective-permute-start | bytes 1769480 | tf_op jit(solution)/shard_map/ppermute | solution.py:15
  94.7 18.9 %collective-permute-start.1 = (bf16[2,384,384]{2,1,0:T(8,128)(2,1)}, bf16[2,384,384]{2,1,0:T(8,128)(2,1)}, u32[]{:S(2)}, u32[]{:S(2)}) collective-permute-start(bf16[2,384,384]{2,1,0:T(8,128)(2,1)} %pad_maximum_fusion), channel_id=1, source_target_pairs={{0,24},{8,32},{16,40},{24,48},{32,56},{40,64},{48,72},{56,80},{64,... | collective-permute-start | bytes 1769480 | tf_op jit(solution)/shard_map/ppermute | solution.py:15
  95.0 66.3 %collective-permute-start.7 = (bf16[2,384,384]{2,1,0:T(8,128)(2,1)}, bf16[2,384,384]{2,1,0:T(8,128)(2,1)}, u32[]{:S(2)}, u32[]{:S(2)}) collective-permute-start(bf16[2,384,384]{2,1,0:T(8,128)(2,1)} %pad_maximum_fusion), channel_id=1, source_target_pairs={{0,224},{8,232},{16,240},{24,248},{32,0},{40,8},{48,16},{56,24},{6... | collective-permute-start | bytes 1769480 | tf_op jit(solution)/shard_map/ppermute | solution.py:15
  96.9 46.2 %collective-permute-start.3 = (bf16[2,384,384]{2,1,0:T(8,128)(2,1)}, bf16[2,384,384]{2,1,0:T(8,128)(2,1)}, u32[]{:S(2)}, u32[]{:S(2)}) collective-permute-start(bf16[2,384,384]{2,1,0:T(8,128)(2,1)} %pad_maximum_fusion), channel_id=1, source_target_pairs={{0,8},{8,16},{16,24},{24,32},{32,40},{40,48},{48,56},{56,64},{64,7... | collective-permute-start | bytes 1769480 | tf_op jit(solution)/shard_map/ppermute | solution.py:15
  98.2 39.6 %collective-permute-start.2 = (bf16[2,384,384]{2,1,0:T(8,128)(2,1)}, bf16[2,384,384]{2,1,0:T(8,128)(2,1)}, u32[]{:S(2)}, u32[]{:S(2)}) collective-permute-start(bf16[2,384,384]{2,1,0:T(8,128)(2,1)} %pad_maximum_fusion), channel_id=1, source_target_pairs={{0,16},{8,24},{16,32},{24,40},{32,48},{40,56},{48,64},{56,72},{64,... | collective-permute-start | bytes 1769480 | tf_op jit(solution)/shard_map/ppermute | solution.py:15
  109.5 34.8 %collective-permute-start.4 = (bf16[2,384,384]{2,1,0:T(8,128)(2,1)}, bf16[2,384,384]{2,1,0:T(8,128)(2,1)S(1)}, u32[]{:S(2)}, u32[]{:S(2)}) collective-permute-start(bf16[2,384,384]{2,1,0:T(8,128)(2,1)} %pad_maximum_fusion), channel_id=1, source_target_pairs={{0,248},{8,0},{16,8},{24,16},{32,24},{40,32},{48,40},{56,48},{64,5... | collective-permute-start | bytes 1769480 | tf_op jit(solution)/shard_map/ppermute | solution.py:15
  113.7 44.6 %collective-permute-start.5 = (bf16[2,384,384]{2,1,0:T(8,128)(2,1)}, bf16[2,384,384]{2,1,0:T(8,128)(2,1)S(1)}, u32[]{:S(2)}, u32[]{:S(2)}) collective-permute-start(bf16[2,384,384]{2,1,0:T(8,128)(2,1)} %pad_maximum_fusion), channel_id=1, source_target_pairs={{0,240},{8,248},{16,0},{24,8},{32,16},{40,24},{48,32},{56,40},{64,... | collective-permute-start | bytes 1769480 | tf_op jit(solution)/shard_map/ppermute | solution.py:15
  137.8 23.5 %collective-permute-start.6 = (bf16[2,384,384]{2,1,0:T(8,128)(2,1)}, bf16[2,384,384]{2,1,0:T(8,128)(2,1)S(1)}, u32[]{:S(2)}, u32[]{:S(2)}) collective-permute-start(bf16[2,384,384]{2,1,0:T(8,128)(2,1)} %pad_maximum_fusion), channel_id=1, source_target_pairs={{0,232},{8,240},{16,248},{24,0},{32,8},{40,16},{48,24},{56,32},{64... | collective-permute-start | bytes 1769480 | tf_op jit(solution)/shard_map/ppermute | solution.py:15
  165.4 9.1 %copy-start.3 = (f32[128]{0:T(128)S(1)}, f32[128]{0:T(128)}, u32[]{:S(2)}) copy-start(f32[128]{0:T(128)} %param.9) | copy-start | bytes 1540
  180.2 4.3 %copy-start.1 = (bf16[1,3456,384]{1,2,0:T(8,128)(2,1)S(1)}, bf16[1,3456,384]{1,2,0:T(8,128)(2,1)}, u32[]{:S(2)}) copy-start(bf16[1,3456,384]{1,2,0:T(8,128)(2,1)} %copy.34) | copy-start | bytes 7962628
Sparse Core Ops, SparseCore 0:
  9.8 67.0 all-gather.1
  196.5 82.5 reduce-scatter.3
where the time goes:
time: 289 us; the launch traced here: 288 us
  waiting for transfers between devices  187 us (65%)
  local copies, waits for them, and re-layouts  40 us (14%)
  matrix products  20.2 us (7%)
  starting transfers between devices  17.7 us (6%)
  between operations  13.6 us (5%)
  other arithmetic  9.58 us (3%)
    unnamed x3, waiting for transfers between devices  83.4 us
    all_gather x1, waiting for transfers between devices, on_device(): lax.all_gather(tokens, 'mp', axis=1, tiled=True)  59.3 us
    ppermute x8, waiting for transfers between devices, passed_along(): return lax.ppermute(value, axis, pairs)  43.9 us
    unnamed x24, local copies, waits for them, and re-layouts  22.5 us
    ppermute x8, starting transfers between devices, passed_along(): return lax.ppermute(value, axis, pairs)  17.7 us
    slice x2, local copies, waits for them, and re-layouts, on_device(): near_keys = window[0].reshape(window_tiles * TILE, heads_here, HD)  7.38 us
    dot_general x1, matrix products, on_device(): jnp.dot(lax.all_gather(tokens, 'mp', axis=1, tiled=True), flat_w, preferr...  6.96 us
  transfers between devices with their start and end apart: 10, of which 7 were waited for; matrix products, arithmetic and copies ran while one was open for 6% of the time, Pallas kernels for 0%

commit v1 on v0

--- a/solution.py
+++ b/solution.py
@@ -30,7 +30,11 @@
     span_here = (REACH + tiles_here - 1) // tiles_here
     flat_w = w_qkv.reshape(w_qkv.shape[0], 3 * columns)
     projected = jnp.dot(
-        lax.all_gather(tokens, "mp", axis=1, tiled=True), flat_w, preferred_element_type=jnp.float32
+        jnp.concatenate(
+            lax.all_to_all(jnp.stack([tokens] * lax.axis_size("mp")), "mp", 0, 0), axis=1
+        ),
+        flat_w,
+        preferred_element_type=jnp.float32,
     )
     queries = head_norm(projected[:, :columns], q_gain)
     key_part = head_norm(projected[:, columns : 2 * columns], k_gain).reshape(tok_rows, columns)

time: 289 us -> 264 us (0.913)
  waiting for transfers between devices: 187 us -> 148 us
  starting transfers between devices: 17.7 us -> 29.1 us
    all_gather x1 -> x0, waiting for transfers between devices: 59.3 us -> none  [on_device(): lax.all_gather(tokens, 'mp', axis=1, tiled=True)]
    all_to_all x0 -> x1, waiting for transfers between devices: none -> 19.9 us  [on_device(): lax.all_to_all(jnp.stack([tokens] * lax.axis_size('mp')), 'mp', 0, 0)]
    all_to_all x0 -> x1, starting transfers between devices: none -> 7.46 us  [on_device(): lax.all_to_all(jnp.stack([tokens] * lax.axis_size('mp')), 'mp', 0, 0)]
    ppermute x8, starting transfers between devices: 17.7 us -> 21.6 us  [passed_along(): return lax.ppermute(value, axis, pairs)]
    unnamed x3 -> x2, waiting for transfers between devices: 83.4 us -> 85.1 us
    unnamed x24 -> x25, local copies, waits for them, and re-layouts: 22.5 us -> 23.8 us
  transfers between devices with their start and end apart: 10 -> 10, of which waited for: 7 -> 7; matrix products, arithmetic and copies ran while one was open for 6% -> 7% of each run, Pallas kernels for 0% -> 0%
where the time goes in v1:
time: 264 us; the launch traced here: 263 us
  waiting for transfers between devices  148 us (56%)
  local copies, waits for them, and re-layouts  42.8 us (16%)
  starting transfers between devices  29.1 us (11%)
  matrix products  20.2 us (8%)
  between operations  13.6 us (5%)
  other arithmetic  9.56 us (4%)
    unnamed x2, waiting for transfers between devices  85.1 us
    ppermute x8, waiting for transfers between devices, passed_along(): return lax.ppermute(value, axis, pairs)  42.6 us
    unnamed x25, local copies, waits for them, and re-layouts  23.8 us
    ppermute x8, starting transfers between devices, passed_along(): return lax.ppermute(value, axis, pairs)  21.6 us
    all_to_all x1, waiting for transfers between devices, on_device(): lax.all_to_all(jnp.stack([tokens] * lax.axis_size('mp')), 'mp', 0, 0)  19.9 us
    all_to_all x1, starting transfers between devices, on_device(): lax.all_to_all(jnp.stack([tokens] * lax.axis_size('mp')), 'mp', 0, 0)  7.46 us
    slice x2, local copies, waits for them, and re-layouts, on_device(): near_keys = window[0].reshape(window_tiles * TILE, heads_here, HD)  7.36 us
    dot_general x1, matrix products, on_device(): jnp.dot(jnp.concatenate(lax.all_to_all(jnp.stack([tokens] * lax.axis_size...  6.97 us
  transfers between devices with their start and end apart: 10, of which 7 were waited for; matrix products, arithmetic and copies ran while one was open for 7% of the time, Pallas kernels for 0%

profile of v1, /device:TPU:2, one launch (start us, length us, event | category | flops | bytes accessed | tf_op | source)
XLA Modules:
  0.0 262.8 jit_solution(15700486403941618136)
XLA Ops:
  6.5 0.0 copy-start
  6.5 1.3 copy.33
  7.9 1.6 stack.6
  9.5 7.5 %all-to-all-start = ((bf16[8,384,384]{1,2,0:T(8,128)(2,1)}), bf16[8,384,384]{1,2,0:T(8,128)(2,1)}, u32[]{:S(2)}, u32[]{:S(2)}) async-start(bf16[8,384,384]{1,2,0:T(8,128)(2,1)} %stack.6), calls=%async_computation | async-start | bytes 4718592 | tf_op jit(solution)/shard_map/all_to_all | solution.py:34
  16.9 0.0 reduce-scatter.4.cloned.1.call-start
  16.9 10.3 %copy.34 = bf16[3072,3,384]{0,2,1:T(8,128)(2,1)} copy(bf16[3072,3,384]{2,0,1:T(8,128)(2,1)} %param.8) | data formatting | bytes 14155776 | tf_op args[1]
  27.2 0.0 copy-done.5
  27.2 19.9 %all-to-all-done = bf16[8,384,384]{1,2,0:T(8,128)(2,1)} async-done(((bf16[8,384,384]{1,2,0:T(8,128)(2,1)}), bf16[8,384,384]{1,2,0:T(8,128)(2,1)}, u32[]{:S(2)}, u32[]{:S(2)}) %all-to-all-start) | async-done | bytes 2359328 | tf_op jit(solution)/shard_map/all_to_all | solution.py:34
  47.1 7.0 %fusion.21 = f32[384,1152]{1,0:T(8,128)S(1)} fusion(bf16[384,3072]{0,1:T(8,128)(2,1)} %bitcast.1, bf16[3072,1152]{0,1:T(8,128)(2,1)} %bitcast.66), kind=kOutput, calls=%fused_computation.47 | convolution fusion | flops 2717908992 | bytes 11206656 | tf_op jit(solution)/shard_map/dot_general | solution.py:32
  54.1 0.0 copy-start.2
  54.1 0.0 copy-start.6
  54.1 0.0 copy-start.4
  54.2 1.2 copy-done.2
  55.3 0.9 slice_multiply_fusion
  56.2 1.3 copy.35
  57.6 1.1 copy.36
  58.7 2.4 fusion.20
  61.0 0.9 pad_maximum_fusion
  61.9 1.9 collective-permute-start
  63.8 0.0 copy-done.6
  63.8 0.6 dynamic_slice.7
  64.4 0.0 copy-done.4
  64.4 0.2 fusion.14
  64.6 0.7 iota_compare_fusion.1
  65.3 0.1 collective-permute-start.1
  65.4 0.1 fusion.16
  65.4 0.1 broadcast_in_dim.12
  65.5 4.0 %collective-permute-start.7 = (bf16[2,384,384]{2,1,0:T(8,128)(2,1)}, bf16[2,384,384]{2,1,0:T(8,128)(2,1)}, u32[]{:S(2)}, u32[]{:S(2)}) collective-permute-start(bf16[2,384,384]{2,1,0:T(8,128)(2,1)} %pad_maximum_fusion), channel_id=1, source_target_pairs={{0,224},{8,232},{16,240},{24,248},{32,0},{40,8},{48,16},{56,24},{6... | collective-permute-start | bytes 1769480 | tf_op jit(solution)/shard_map/ppermute | solution.py:15
  69.6 0.0 collective-permute-start.3
  69.6 0.7 collective-permute-start.2
  70.2 1.3 copy.39
  71.5 0.1 multiply_reduce_fusion
  71.6 10.6 %collective-permute-done = bf16[2,384,384]{2,1,0:T(8,128)(2,1)} collective-permute-done((bf16[2,384,384]{2,1,0:T(8,128)(2,1)}, bf16[2,384,384]{2,1,0:T(8,128)(2,1)}, u32[]{:S(2)}, u32[]{:S(2)}) %collective-permute-start) | collective-permute-done | bytes 589856 | tf_op jit(solution)/shard_map/ppermute | solution.py:15
  82.3 0.0 collective-permute-start.4
  82.3 1.1 constant_dynamic-update-slice_fusion.8
  83.4 3.2 %collective-permute-done.1 = bf16[2,384,384]{2,1,0:T(8,128)(2,1)} collective-permute-done((bf16[2,384,384]{2,1,0:T(8,128)(2,1)}, bf16[2,384,384]{2,1,0:T(8,128)(2,1)}, u32[]{:S(2)}, u32[]{:S(2)}) %collective-permute-start.1) | collective-permute-done | bytes 589856 | tf_op jit(solution)/shard_map/ppermute | solution.py:15
  86.6 8.0 %collective-permute-start.5 = (bf16[2,384,384]{2,1,0:T(8,128)(2,1)}, bf16[2,384,384]{2,1,0:T(8,128)(2,1)S(1)}, u32[]{:S(2)}, u32[]{:S(2)}) collective-permute-start(bf16[2,384,384]{2,1,0:T(8,128)(2,1)} %pad_maximum_fusion), channel_id=1, source_target_pairs={{0,240},{8,248},{16,0},{24,8},{32,16},{40,24},{48,32},{56,40},{64,... | collective-permute-start | bytes 1769480 | tf_op jit(solution)/shard_map/ppermute | solution.py:15
  94.6 1.2 constant_dynamic-update-slice_fusion.7
  95.8 12.0 %collective-permute-done.2 = bf16[2,384,384]{2,1,0:T(8,128)(2,1)} collective-permute-done((bf16[2,384,384]{2,1,0:T(8,128)(2,1)}, bf16[2,384,384]{2,1,0:T(8,128)(2,1)}, u32[]{:S(2)}, u32[]{:S(2)}) %collective-permute-start.2) | collective-permute-done | bytes 589856 | tf_op jit(solution)/shard_map/ppermute | solution.py:15
  107.7 6.9 %collective-permute-start.6 = (bf16[2,384,384]{2,1,0:T(8,128)(2,1)}, bf16[2,384,384]{2,1,0:T(8,128)(2,1)S(1)}, u32[]{:S(2)}, u32[]{:S(2)}) collective-permute-start(bf16[2,384,384]{2,1,0:T(8,128)(2,1)} %pad_maximum_fusion), channel_id=1, source_target_pairs={{0,232},{8,240},{16,248},{24,0},{32,8},{40,16},{48,24},{56,32},{64... | collective-permute-start | bytes 1769480 | tf_op jit(solution)/shard_map/ppermute | solution.py:15
  114.7 1.2 constant_dynamic-update-slice_fusion.6
  115.8 0.0 collective-permute-done.3
  115.8 1.2 constant_dynamic-update-slice_fusion.5
  117.0 0.1 constant_dynamic-update-slice_fusion.4
  117.1 0.0 collective-permute-done.4
  117.1 0.1 constant_dynamic-update-slice_fusion.3
  117.2 13.6 %collective-permute-done.5 = bf16[2,384,384]{2,1,0:T(8,128)(2,1)S(1)} collective-permute-done((bf16[2,384,384]{2,1,0:T(8,128)(2,1)}, bf16[2,384,384]{2,1,0:T(8,128)(2,1)S(1)}, u32[]{:S(2)}, u32[]{:S(2)}) %collective-permute-start.5) | collective-permute-done | bytes 589856 | tf_op jit(solution)/shard_map/ppermute | solution.py:15
  130.8 0.1 constant_dynamic-update-slice_fusion.2
  130.9 3.1 %collective-permute-done.6 = bf16[2,384,384]{2,1,0:T(8,128)(2,1)S(1)} collective-permute-done((bf16[2,384,384]{2,1,0:T(8,128)(2,1)}, bf16[2,384,384]{2,1,0:T(8,128)(2,1)S(1)}, u32[]{:S(2)}, u32[]{:S(2)}) %collective-permute-start.6) | collective-permute-done | bytes 589856 | tf_op jit(solution)/shard_map/ppermute | solution.py:15
  134.0 0.1 constant_dynamic-update-slice_fusion.1
  134.1 0.0 collective-permute-done.7
  134.1 1.2 constant_dynamic-update-slice_fusion
  135.3 2.8 %fusion.19 = (bf16[1,3456,384]{2,1,0:T(8,128)(2,1)}, bf16[1,3456,384]{2,1,0:T(8,128)(2,1)}) fusion(bf16[2,3456,384]{2,1,0:T(8,128)(2,1)S(1)} %constant_dynamic-update-slice_fusion), kind=kLoop, calls=%fused_computation.45 | loop fusion | bytes 10616832 | tf_op jit(solution)/shard_map/slice | solution.py:64
  138.2 4.5 %copy.38 = bf16[1,3456,384]{1,2,0:T(8,128)(2,1)} copy(bf16[1,3456,384]{2,1,0:T(8,128)(2,1)} %get-tuple-element.5) | data formatting | bytes 5308416 | tf_op jit(solution)/shard_map/slice | solution.py:64
  142.7 4.5 %copy.37 = bf16[1,3456,384]{1,2,0:T(8,128)(2,1)} copy(bf16[1,3456,384]{2,1,0:T(8,128)(2,1)} %get-tuple-element.6) | data formatting | bytes 5308416 | tf_op jit(solution)/shard_map/slice | solution.py:65
  147.1 5.7 %bitcast_reduce_fusion = (f32[3,384]{1,0:T(4,128)S(1)}, f32[3,3456,384]{2,1,0:T(8,128)S(1)}) fusion(pred[3456]{0:T(1024)(128)(4,1)S(1)} %broadcast_in_dim.13, bf16[3456,3,128]{0,2,1:T(8,128)(2,1)} %bitcast.65, f32[384,3,128]{0,2,1:T(8,128)S(1)} %bitcast.68, f32[128]{0:T(128)S(1)} %copy-done.3, f32[384,3]{0,1:T(4,128)S(1)} %add_rsqrt_fusion), kind=kOutput, calls=%fused_computation.1 | convolution fusion | flops 1031601024 | bytes 19182464 | tf_op jit(solution)/shard_map/tqhd,khd->thqk/dot_general | solution.py:67
  152.9 4.3 %fusion.1 = f32[3,384]{1,0:T(4,128)S(1)} fusion(f32[3,3456,384]{2,1,0:T(8,128)S(1)} %get-tuple-element.10, f32[3,384]{1,0:T(4,128)S(1)} %get-tuple-element.9, pred[3456]{0:T(1024)(128)(4,1)S(1)} %broadcast_in_dim.13), kind=kLoop, calls=%fused_computation.5 | loop fusion | flops 15924096 | bytes 15937920 | tf_op jit(solution)/shard_map/reduce_sum | solution.py:73
  157.2 0.0 copy-done.1
  157.2 4.7 %fusion.5 = bf16[3,128,384]{2,1,0:T(8,128)(2,1)S(1)} fusion(bf16[3456,3,128]{0,2,1:T(8,128)(2,1)S(1)} %bitcast.69, f32[3,384]{1,0:T(4,128)S(1)} %fusion.1, f32[3,384]{1,0:T(4,128)S(1)} %get-tuple-element.9, f32[3,3456,384]{2,1,0:T(8,128)S(1)} %get-tuple-element.10, pred[3456]{0:T(1024)(128)(4,1)S(1)} %broadcast_in_dim.13), kind=kOutput, calls=%fused_computation.10 | convolution fusion | flops 1039269888 | bytes 18887040 | tf_op jit(solution)/shard_map/thqk,khd->tqhd/dot_general | solution.py:74
  161.9 2.8 %fusion.4 = bf16[3072,384]{0,1:T(8,128)(2,1)} fusion(bf16[384,384]{0,1:T(8,128)(2,1)S(1)} %bitcast.72, bf16[384,3072]{1,0:T(8,128)(2,1)S(1)} %copy-done), kind=kOutput, calls=%fused_computation.9 | convolution fusion | flops 907149312 | bytes 5013504 | tf_op jit(solution)/shard_map/dot_general | solution.py:77
  164.7 4.3 %copy.46 = bf16[3072,384]{1,0:T(8,128)(2,1)} copy(bf16[3072,384]{0,1:T(8,128)(2,1)} %fusion.4) | data formatting | bytes 4718592
  169.0 0.0 reduce-scatter.4.cloned.1.call-update
  169.1 85.1 %reduce-scatter.4.cloned.1.call-done = bf16[384,384]{1,0:T(8,128)(2,1)} async-done(((bf16[3072,384]{1,0:T(8,128)(2,1)}), bf16[384,384]{1,0:T(8,128)(2,1)}) %reduce-scatter.4.cloned.1.call-update) | async-done | bytes 294928
  254.1 1.8 copy.47
  (12 shorter events, 0.2 us)
Async XLA Ops:
  6.5 155.4 %copy-start = (bf16[384,3072]{1,0:T(8,128)(2,1)S(1)}, bf16[384,3072]{1,0:T(8,128)(2,1)}, u32[]{:S(2)}) copy-start(bf16[384,3072]{1,0:T(8,128)(2,1)} %param.11) | copy-start | bytes 7077892
  9.5 37.6 %all-to-all-start = ((bf16[8,384,384]{1,2,0:T(8,128)(2,1)}), bf16[8,384,384]{1,2,0:T(8,128)(2,1)}, u32[]{:S(2)}, u32[]{:S(2)}) async-start(bf16[8,384,384]{1,2,0:T(8,128)(2,1)} %stack.6), calls=%async_computation | async-start | bytes 4718592 | tf_op jit(solution)/shard_map/all_to_all | solution.py:34
  16.9 10.3 %copy-start.5 = (f32[128]{0:T(128)S(1)}, f32[128]{0:T(128)}, u32[]{:S(2)}) copy-start(f32[128]{0:T(128)} %param.10) | copy-start | bytes 1540
  16.9 237.2 %reduce-scatter.4.cloned.1.call-start = ((), (), s32[]{:S(2)}) async-start(), calls=%async_computation.2 | async-start | bytes 2654208
  54.1 1.2 copy-start.2
  54.1 9.7 %copy-start.6 = (s32[32]{0:T(128)S(1)}, s32[32]{0:T(128)}, u32[]{:S(2)}) copy-start(s32[32]{0:T(128)} %param.13) | copy-start | bytes 388
  54.1 10.3 %copy-start.4 = (s32[32,6]{0,1:T(8,128)S(1)}, s32[32,6]{0,1:T(8,128)}, u32[]{:S(2)}) copy-start(s32[32,6]{0,1:T(8,128)} %param.12) | copy-start | bytes 2308
  61.9 20.3 %collective-permute-start = (bf16[2,384,384]{2,1,0:T(8,128)(2,1)}, bf16[2,384,384]{2,1,0:T(8,128)(2,1)}, u32[]{:S(2)}, u32[]{:S(2)}) collective-permute-start(bf16[2,384,384]{2,1,0:T(8,128)(2,1)} %pad_maximum_fusion), channel_id=1, source_target_pairs={{0,32},{8,40},{16,48},{24,56},{32,64},{40,72},{48,80},{56,88},{64,... | collective-permute-start | bytes 1769480 | tf_op jit(solution)/shard_map/ppermute | solution.py:15
  65.3 21.3 %collective-permute-start.1 = (bf16[2,384,384]{2,1,0:T(8,128)(2,1)}, bf16[2,384,384]{2,1,0:T(8,128)(2,1)}, u32[]{:S(2)}, u32[]{:S(2)}) collective-permute-start(bf16[2,384,384]{2,1,0:T(8,128)(2,1)} %pad_maximum_fusion), channel_id=1, source_target_pairs={{0,24},{8,32},{16,40},{24,48},{32,56},{40,64},{48,72},{56,80},{64,... | collective-permute-start | bytes 1769480 | tf_op jit(solution)/shard_map/ppermute | solution.py:15
  65.5 68.6 %collective-permute-start.7 = (bf16[2,384,384]{2,1,0:T(8,128)(2,1)}, bf16[2,384,384]{2,1,0:T(8,128)(2,1)}, u32[]{:S(2)}, u32[]{:S(2)}) collective-permute-start(bf16[2,384,384]{2,1,0:T(8,128)(2,1)} %pad_maximum_fusion), channel_id=1, source_target_pairs={{0,224},{8,232},{16,240},{24,248},{32,0},{40,8},{48,16},{56,24},{6... | collective-permute-start | bytes 1769480 | tf_op jit(solution)/shard_map/ppermute | solution.py:15
  69.6 46.2 %collective-permute-start.3 = (bf16[2,384,384]{2,1,0:T(8,128)(2,1)}, bf16[2,384,384]{2,1,0:T(8,128)(2,1)}, u32[]{:S(2)}, u32[]{:S(2)}) collective-permute-start(bf16[2,384,384]{2,1,0:T(8,128)(2,1)} %pad_maximum_fusion), channel_id=1, source_target_pairs={{0,8},{8,16},{16,24},{24,32},{32,40},{40,48},{48,56},{56,64},{64,7... | collective-permute-start | bytes 1769480 | tf_op jit(solution)/shard_map/ppermute | solution.py:15
  69.6 38.2 %collective-permute-start.2 = (bf16[2,384,384]{2,1,0:T(8,128)(2,1)}, bf16[2,384,384]{2,1,0:T(8,128)(2,1)}, u32[]{:S(2)}, u32[]{:S(2)}) collective-permute-start(bf16[2,384,384]{2,1,0:T(8,128)(2,1)} %pad_maximum_fusion), channel_id=1, source_target_pairs={{0,16},{8,24},{16,32},{24,40},{32,48},{40,56},{48,64},{56,72},{64,... | collective-permute-start | bytes 1769480 | tf_op jit(solution)/shard_map/ppermute | solution.py:15
  82.3 34.8 %collective-permute-start.4 = (bf16[2,384,384]{2,1,0:T(8,128)(2,1)}, bf16[2,384,384]{2,1,0:T(8,128)(2,1)S(1)}, u32[]{:S(2)}, u32[]{:S(2)}) collective-permute-start(bf16[2,384,384]{2,1,0:T(8,128)(2,1)} %pad_maximum_fusion), channel_id=1, source_target_pairs={{0,248},{8,0},{16,8},{24,16},{32,24},{40,32},{48,40},{56,48},{64,5... | collective-permute-start | bytes 1769480 | tf_op jit(solution)/shard_map/ppermute | solution.py:15
  86.6 44.2 %collective-permute-start.5 = (bf16[2,384,384]{2,1,0:T(8,128)(2,1)}, bf16[2,384,384]{2,1,0:T(8,128)(2,1)S(1)}, u32[]{:S(2)}, u32[]{:S(2)}) collective-permute-start(bf16[2,384,384]{2,1,0:T(8,128)(2,1)} %pad_maximum_fusion), channel_id=1, source_target_pairs={{0,240},{8,248},{16,0},{24,8},{32,16},{40,24},{48,32},{56,40},{64,... | collective-permute-start | bytes 1769480 | tf_op jit(solution)/shard_map/ppermute | solution.py:15
  107.7 26.3 %collective-permute-start.6 = (bf16[2,384,384]{2,1,0:T(8,128)(2,1)}, bf16[2,384,384]{2,1,0:T(8,128)(2,1)S(1)}, u32[]{:S(2)}, u32[]{:S(2)}) collective-permute-start(bf16[2,384,384]{2,1,0:T(8,128)(2,1)} %pad_maximum_fusion), channel_id=1, source_target_pairs={{0,232},{8,240},{16,248},{24,0},{32,8},{40,16},{48,24},{56,32},{64... | collective-permute-start | bytes 1769480 | tf_op jit(solution)/shard_map/ppermute | solution.py:15
  138.2 9.0 %copy-start.3 = (f32[128]{0:T(128)S(1)}, f32[128]{0:T(128)}, u32[]{:S(2)}) copy-start(f32[128]{0:T(128)} %param.9) | copy-start | bytes 1540
  152.9 4.3 %copy-start.1 = (bf16[1,3456,384]{1,2,0:T(8,128)(2,1)S(1)}, bf16[1,3456,384]{1,2,0:T(8,128)(2,1)}, u32[]{:S(2)}) copy-start(bf16[1,3456,384]{1,2,0:T(8,128)(2,1)} %copy.37) | copy-start | bytes 7962628
Sparse Core Ops, SparseCore 0:
  169.2 84.8 reduce-scatter.3
